TPU v7x, 256 devices: a whole 4x4x8 slice. The times are simulated.
256 devices in a mesh: prow: 8 (over z_hi, core), pcol: 32 (over x, z_lo, y).
Axes of the slice: x: 4, y: 4, z: 8 (z_hi: 4, z_lo: 2; z = z_hi * 2 + z_lo), core: 2. Of those that a mesh axis runs over, the one named last changes fastest.
Arguments:
- slab: float32 [2048, 98304], P('pcol', 'prow'), may hold values from -6 to 6
- vectors: float32 [98304, 512], P(('prow', 'pcol')), may hold values from -0.01953125 to 0.01953125
- tfactors: float32 [4, 128, 128], replicated, as said below
Outputs:
- transformed: float32 [2048, 98304], P('pcol', 'prow')
Inputs may be any that keep to these rules, and one draw needn't show every extreme that they name: Each tfactors[k] is upper triangular with diagonal entries between 1 and 2.
All inputs are finite; a program needn't handle non-finite values.
Results may differ from a plain program's by a relative error of at most 0.0001.
Values sent between devices are 32-bit elements; how exact they have to be, the bound alone decides.
No kernel may reach another device: no remote copies, remote signals or barrier semaphores. Data moves between devices by JAX's collectives and lax.ppermute only.
A program may use at most 128 MiB of HBM per device.

v0:
```python
import jax
import jax.numpy as jnp
from jax import lax
from jax.sharding import PartitionSpec as P


def matmul(left, right):
    return jnp.dot(left, right, precision=lax.Precision.HIGHEST, preferred_element_type=jnp.float32)


def per_device(slab, vectors, tfactors):
    count = tfactors.shape[0]
    width = tfactors.shape[1]
    work = slab
    for k in reversed(range(count)):
        basis = lax.all_gather(vectors[:, k * width : (k + 1) * width], "pcol", axis=0, tiled=True)
        products = lax.psum(matmul(work, basis), "prow")
        work = work - matmul(matmul(products, tfactors[k].T), basis.T)
    return work


def solution(mesh):
    in_specs = (P("pcol", "prow"), P(("prow", "pcol"), None), P())
    out_specs = P("pcol", "prow")
    return jax.shard_map(
        per_device, mesh=mesh, in_specs=in_specs, out_specs=out_specs, check_vma=False
    )
```

profile of v0, /device:TPU:8, one launch (start us, length us, event | category | flops | bytes accessed | tf_op | source)
XLA Modules:
  0.0 729.5 jit_solution(4784247094145726816)
XLA Ops:
  6.5 0.0 all-gather.5.cloned.1.call-start
  6.5 2.1 fusion.12
  8.6 0.0 all-gather.5.cloned.1.call-update
  8.7 0.0 all-gather.7.cloned.1.call-start
  8.7 0.7 all-gather.7.cloned.1.call-update
  9.4 0.0 all-gather.9.cloned.1.call-start
  9.5 0.7 all-gather.9.cloned.1.call-update
  10.2 0.0 all-gather.11.cloned.1.call-start
  10.2 0.5 all-gather.11.cloned.1.call-update
  10.7 0.0 copy-start.2
  10.7 166.6 %all-gather.5.cloned.1.call-done = f32[12288,128]{1,0:T(8,128)} async-done(((f32[384,128]{1,0:T(8,128)}), f32[12288,128]{1,0:T(8,128)}) %all-gather.5.cloned.1.call-update) | async-done | bytes 6291472 | tf_op jit(solution)/shard_map/all_gather | solution.py:16
  177.3 6.4 fusion.13
  183.8 27.2 %psum.28 = f32[64,128]{1,0:T(8,128)S(1)} all-reduce(f32[64,128]{1,0:T(8,128)S(1)} %fusion.13), channel_id=1, replica_groups=mesh['prow'=8,'pcol'=32] {'prow'}, use_global_device_ids=true, to_apply=%region_0.0 | all-reduce | flops 8192 | bytes 65536 | tf_op jit(solution)/shard_map/psum | solution.py:17
  211.0 0.0 copy-done.2
  211.0 0.2 fusion.6
  211.2 9.4 %convolution_subtract_fusion.3 = f32[64,12288]{1,0:T(8,128)S(1)} fusion(f32[64,12288]{1,0:T(8,128)} %param.3, f32[64,128]{1,0:T(8,128)S(1)} %fusion.6, f32[12288,128]{1,0:T(8,128)} %all-gather.5.cloned.1.call-done), kind=kOutput, calls=%fused_computation.3 | convolution fusion | flops 1208745984 | bytes 12615680 | tf_op jit(solution)/shard_map/dot_general | solution.py:8
  220.6 0.0 copy-start.1
  220.6 124.5 %all-gather.7.cloned.1.call-done = f32[12288,128]{1,0:T(8,128)} async-done(((f32[384,128]{1,0:T(8,128)}), f32[12288,128]{1,0:T(8,128)}) %all-gather.7.cloned.1.call-update) | async-done | bytes 6291472 | tf_op jit(solution)/shard_map/all_gather | solution.py:16
  345.1 5.9 fusion.14
  351.1 0.0 copy-done.1
  351.1 27.4 %psum.29 = f32[64,128]{1,0:T(8,128)S(1)} all-reduce(f32[64,128]{1,0:T(8,128)S(1)} %fusion.14), channel_id=1, replica_groups=mesh['prow'=8,'pcol'=32] {'prow'}, use_global_device_ids=true, to_apply=%region_1.0 | all-reduce | flops 8192 | bytes 65536 | tf_op jit(solution)/shard_map/psum | solution.py:17
  378.4 0.2 fusion.4
  378.7 9.4 %convolution_subtract_fusion.2 = f32[64,12288]{1,0:T(8,128)S(1)} fusion(f32[64,12288]{1,0:T(8,128)} %copy-done.1, f32[64,128]{1,0:T(8,128)S(1)} %fusion.4, f32[12288,128]{1,0:T(8,128)} %all-gather.7.cloned.1.call-done), kind=kOutput, calls=%fused_computation.2 | convolution fusion | flops 1208745984 | bytes 12615680 | tf_op jit(solution)/shard_map/dot_general | solution.py:8
  388.1 123.8 %all-gather.9.cloned.1.call-done = f32[12288,128]{1,0:T(8,128)} async-done(((f32[384,128]{1,0:T(8,128)}), f32[12288,128]{1,0:T(8,128)}) %all-gather.9.cloned.1.call-update) | async-done | bytes 6291472 | tf_op jit(solution)/shard_map/all_gather | solution.py:16
  511.9 5.9 fusion.15
  517.8 27.2 %psum.30 = f32[64,128]{1,0:T(8,128)S(1)} all-reduce(f32[64,128]{1,0:T(8,128)S(1)} %fusion.15), channel_id=1, replica_groups=mesh['prow'=8,'pcol'=32] {'prow'}, use_global_device_ids=true, to_apply=%region_2.0 | all-reduce | flops 8192 | bytes 65536 | tf_op jit(solution)/shard_map/psum | solution.py:17
  545.0 0.2 fusion.2
  545.3 10.1 %convolution_subtract_fusion.1 = f32[64,12288]{1,0:T(8,128)} fusion(f32[64,12288]{1,0:T(8,128)S(1)} %convolution_subtract_fusion.2, f32[64,128]{1,0:T(8,128)S(1)} %fusion.2, f32[12288,128]{1,0:T(8,128)} %all-gather.9.cloned.1.call-done), kind=kOutput, calls=%fused_computation.1 | convolution fusion | flops 1208745984 | bytes 12615680 | tf_op jit(solution)/shard_map/dot_general | solution.py:8
  555.3 0.0 copy-start
  555.3 123.4 %all-gather.11.cloned.1.call-done = f32[12288,128]{1,0:T(8,128)} async-done(((f32[384,128]{1,0:T(8,128)}), f32[12288,128]{1,0:T(8,128)}) %all-gather.11.cloned.1.call-update) | async-done | bytes 6291472 | tf_op jit(solution)/shard_map/all_gather | solution.py:16
  678.7 6.4 fusion.16
  685.1 27.5 %psum.31 = f32[64,128]{1,0:T(8,128)S(1)} all-reduce(f32[64,128]{1,0:T(8,128)S(1)} %fusion.16), channel_id=1, replica_groups=mesh['prow'=8,'pcol'=32] {'prow'}, use_global_device_ids=true, to_apply=%region_3.0 | all-reduce | flops 8192 | bytes 65536 | tf_op jit(solution)/shard_map/psum | solution.py:17
  712.6 0.2 fusion
  712.9 0.0 copy-done
  712.9 10.1 %convolution_subtract_fusion = f32[64,12288]{1,0:T(8,128)} fusion(f32[64,12288]{1,0:T(8,128)S(1)} %copy-done, f32[64,128]{1,0:T(8,128)S(1)} %fusion, f32[12288,128]{1,0:T(8,128)} %all-gather.11.cloned.1.call-done), kind=kOutput, calls=%fused_computation | convolution fusion | flops 1208745984 | bytes 12615680 | tf_op jit(solution)/shard_map/dot_general | solution.py:8
Async XLA Ops:
  6.5 170.8 %all-gather.5.cloned.1.call-start = ((), (), s32[]{:S(2)}) async-start(), calls=%async_computation | async-start | bytes 6488064 | tf_op jit(solution)/shard_map/all_gather | solution.py:16
  8.7 336.4 %all-gather.7.cloned.1.call-start = ((), (), s32[]{:S(2)}) async-start(), calls=%async_computation.1 | async-start | bytes 6488064 | tf_op jit(solution)/shard_map/all_gather | solution.py:16
  9.4 502.5 %all-gather.9.cloned.1.call-start = ((), (), s32[]{:S(2)}) async-start(), calls=%async_computation.2 | async-start | bytes 6488064 | tf_op jit(solution)/shard_map/all_gather | solution.py:16
  10.2 668.5 %all-gather.11.cloned.1.call-start = ((), (), s32[]{:S(2)}) async-start(), calls=%async_computation.3 | async-start | bytes 6488064 | tf_op jit(solution)/shard_map/all_gather | solution.py:16
  10.7 200.2 %copy-start.2 = (f32[4,128,128]{2,1,0:T(8,128)S(1)}, f32[4,128,128]{2,1,0:T(8,128)}, u32[]{:S(2)}) copy-start(f32[4,128,128]{2,1,0:T(8,128)} %param.5) | copy-start | bytes 786436
  220.6 130.4 %copy-start.1 = (f32[64,12288]{1,0:T(8,128)}, f32[64,12288]{1,0:T(8,128)S(1)}, u32[]{:S(2)}) copy-start(f32[64,12288]{1,0:T(8,128)S(1)} %convolution_subtract_fusion.3) | copy-start | bytes 9437188
  555.3 157.5 %copy-start = (f32[64,12288]{1,0:T(8,128)S(1)}, f32[64,12288]{1,0:T(8,128)}, u32[]{:S(2)}) copy-start(f32[64,12288]{1,0:T(8,128)} %convolution_subtract_fusion.1) | copy-start | bytes 9437188
Sparse Core Ops, SparseCore 0:
  9.1 168.1 all-gather.4
  179.1 165.9 all-gather.6
  346.9 164.9 all-gather.8
  513.5 165.1 all-gather.10
where the time goes:
time: 730 us; the launch traced here: 729 us
  waiting for transfers between devices  540 us (74%)
  blocking collectives  109 us (15%)
  matrix products  64.6 us (9%)
  between operations  13.2 us (2%)
    all_gather x4, waiting for transfers between devices, per_device(): lax.all_gather(vectors[:, k * width:(k + 1) * width], 'pcol', axis=0, til...  538 us
    psum x4, blocking collectives, per_device(): products = lax.psum(matmul(work, basis), 'prow')  109 us
    dot_general x12, matrix products, matmul(): jnp.dot(left, right, precision=lax.Precision.HIGHEST, preferred_element_t...  64.6 us
  transfers between devices with their start and end apart: 4, of which 4 were waited for; matrix products, arithmetic and copies ran while one was open for 7% of the time, Pallas kernels for 0%

commit v1 on v0

--- a/solution.py
+++ b/solution.py
@@ -13,7 +13,15 @@
     width = tfactors.shape[1]
     work = slab
     for k in reversed(range(count)):
-        basis = lax.all_gather(vectors[:, k * width : (k + 1) * width], "pcol", axis=0, tiled=True)
+        basis = jnp.concatenate(
+            lax.all_to_all(
+                jnp.stack([vectors[:, k * width : (k + 1) * width]] * lax.axis_size("pcol")),
+                "pcol",
+                0,
+                0,
+            ),
+            axis=0,
+        )
         products = lax.psum(matmul(work, basis), "prow")
         work = work - matmul(matmul(products, tfactors[k].T), basis.T)
     return work

time: 730 us -> 510 us (0.70)
  the two profiles are of different devices: /device:TPU:8 before, /device:TPU:46 now
where the time goes in v1:
time: 510 us
  blocking collectives  429 us (84%)
  matrix products  61 us (12%)
  local copies, waits for them, and re-layouts  10.1 us (2%)
  starting transfers between devices  9.54 us (2%)
    all_to_all x3, blocking collectives, per_device(): lax.all_to_all(jnp.stack([vectors[:, k * width:(k + 1) * width]] * lax.ax...  234 us
    psum x4, blocking collectives, per_device(): products = lax.psum(matmul(work, basis), 'prow')  195 us
    dot_general x12, matrix products, matmul(): jnp.dot(left, right, precision=lax.Precision.HIGHEST, preferred_element_t...  61 us
  transfers between devices with their start and end apart: 1, of which 0 were waited for; matrix products, arithmetic and copies ran while one was open for 9% of the time, Pallas kernels for 0%

profile of v1, /device:TPU:46, one launch (start us, length us, event | category | flops | bytes accessed | tf_op | source)
XLA Modules:
  0.0 509.7 jit_solution(17300750147810188171)
XLA Ops:
  0.0 1.3 fusion.12
  1.3 0.7 stack.8
  2.0 78.6 %all_to_all.20 = f32[32,384,128]{2,1,0:T(8,128)} all-to-all(f32[32,384,128]{2,1,0:T(8,128)S(1)} %stack.8), channel_id=1, replica_groups=mesh['prow'=8,'pcol'=32] {'pcol'}, dimensions={0} | all-to-all | bytes 12582912 | tf_op jit(solution)/shard_map/all_to_all | solution.py:17
  80.6 0.7 stack.9
  81.3 79.7 %all_to_all.21 = f32[32,384,128]{2,1,0:T(8,128)} all-to-all(f32[32,384,128]{2,1,0:T(8,128)S(1)} %stack.9), channel_id=1, replica_groups=mesh['prow'=8,'pcol'=32] {'pcol'}, dimensions={0} | all-to-all | bytes 12582912 | tf_op jit(solution)/shard_map/all_to_all | solution.py:17
  160.9 0.7 stack.10
  161.6 76.1 %all_to_all.22 = f32[32,384,128]{2,1,0:T(8,128)} all-to-all(f32[32,384,128]{2,1,0:T(8,128)S(1)} %stack.10), channel_id=1, replica_groups=mesh['prow'=8,'pcol'=32] {'pcol'}, dimensions={0} | all-to-all | bytes 12582912 | tf_op jit(solution)/shard_map/all_to_all | solution.py:17
  237.7 3.4 stack.11
  241.1 0.0 copy-start.2
  241.1 9.5 %all-to-all-start.3 = ((f32[32,384,128]{2,1,0:T(8,128)}), f32[32,384,128]{2,1,0:T(8,128)}, u32[]{:S(2)}, u32[]{:S(2)}) async-start(f32[32,384,128]{2,1,0:T(8,128)} %stack.11), calls=%async_computation.3 | async-start | bytes 12582912 | tf_op jit(solution)/shard_map/all_to_all | solution.py:17
  250.7 0.0 copy-start.3
  250.7 0.0 copy-done.2
  250.7 6.0 %fusion.13 = f32[64,128]{1,0:T(8,128)S(1)} fusion(f32[64,12288]{1,0:T(8,128)S(1)} %copy-done.2, f32[12288,128]{1,0:T(8,128)} %bitcast.42), kind=kOutput, calls=%fused_computation.17 | convolution fusion | flops 1207959552 | bytes 9469952 | tf_op jit(solution)/shard_map/dot_general | solution.py:8
  256.7 112.4 %psum.28 = f32[64,128]{1,0:T(8,128)S(1)} all-reduce(f32[64,128]{1,0:T(8,128)S(1)} %fusion.13), channel_id=1, replica_groups=mesh['prow'=8,'pcol'=32] {'prow'}, use_global_device_ids=true, to_apply=%region_0.0 | all-reduce | flops 8192 | bytes 65536 | tf_op jit(solution)/shard_map/psum | solution.py:25
  369.1 0.0 copy-done.3
  369.1 0.2 fusion.6
  369.3 8.9 %convolution_subtract_fusion.3 = f32[64,12288]{1,0:T(8,128)S(1)} fusion(f32[64,12288]{1,0:T(8,128)S(1)} %copy-done.2, f32[64,128]{1,0:T(8,128)S(1)} %fusion.6, f32[12288,128]{1,0:T(8,128)} %bitcast.43), kind=kOutput, calls=%fused_computation.3 | convolution fusion | flops 1208745984 | bytes 12615680 | tf_op jit(solution)/shard_map/dot_general | solution.py:8
  378.3 0.0 copy-start.1
  378.3 1.7 copy-done.1
  379.9 0.0 slice-start
  379.9 6.1 %fusion.14 = f32[64,128]{1,0:T(8,128)S(1)} fusion(f32[64,12288]{1,0:T(8,128)S(1)} %convolution_subtract_fusion.3, f32[12288,128]{1,0:T(8,128)} %bitcast.40), kind=kOutput, calls=%fused_computation.18 | convolution fusion | flops 1207959552 | bytes 9469952 | tf_op jit(solution)/shard_map/dot_general | solution.py:8
  386.1 27.4 %psum.29 = f32[64,128]{1,0:T(8,128)S(1)} all-reduce(f32[64,128]{1,0:T(8,128)S(1)} %fusion.14), channel_id=1, replica_groups=mesh['prow'=8,'pcol'=32] {'prow'}, use_global_device_ids=true, to_apply=%region_1.0 | all-reduce | flops 8192 | bytes 65536 | tf_op jit(solution)/shard_map/psum | solution.py:25
  413.5 0.2 fusion.4
  413.7 0.0 slice-start.1
  413.7 9.6 %convolution_subtract_fusion.2 = f32[64,12288]{1,0:T(8,128)S(1)} fusion(f32[64,12288]{1,0:T(8,128)} %copy-done.1, f32[64,128]{1,0:T(8,128)S(1)} %fusion.4, f32[12288,128]{1,0:T(8,128)} %bitcast.41), kind=kOutput, calls=%fused_computation.2 | convolution fusion | flops 1208745984 | bytes 12615680 | tf_op jit(solution)/shard_map/dot_general | solution.py:8
  423.3 0.0 copy-start
  423.3 1.7 copy-done
  425.0 0.0 slice-done
  425.0 0.0 slice-done.1
  425.0 4.0 fusion.15
  429.0 27.5 %psum.30 = f32[64,128]{1,0:T(8,128)S(1)} all-reduce(f32[64,128]{1,0:T(8,128)S(1)} %fusion.15), channel_id=1, replica_groups=mesh['prow'=8,'pcol'=32] {'prow'}, use_global_device_ids=true, to_apply=%region_2.0 | all-reduce | flops 8192 | bytes 65536 | tf_op jit(solution)/shard_map/psum | solution.py:25
  456.5 0.2 fusion.2
  456.7 9.4 %convolution_subtract_fusion.1 = f32[64,12288]{1,0:T(8,128)S(1)} fusion(f32[64,12288]{1,0:T(8,128)} %copy-done, f32[64,128]{1,0:T(8,128)S(1)} %fusion.2, f32[12288,128]{1,0:T(8,128)} %bitcast.36), kind=kOutput, calls=%fused_computation.1 | convolution fusion | flops 1208745984 | bytes 12615680 | tf_op jit(solution)/shard_map/dot_general | solution.py:8
  466.1 0.0 all-to-all-done.3
  466.2 5.9 %fusion.16 = f32[64,128]{1,0:T(8,128)S(1)} fusion(f32[64,12288]{1,0:T(8,128)S(1)} %convolution_subtract_fusion.1, f32[12288,128]{1,0:T(8,128)} %bitcast.6), kind=kOutput, calls=%fused_computation.20 | convolution fusion | flops 1207959552 | bytes 9469952 | tf_op jit(solution)/shard_map/dot_general | solution.py:8
  472.1 27.3 %psum.31 = f32[64,128]{1,0:T(8,128)S(1)} all-reduce(f32[64,128]{1,0:T(8,128)S(1)} %fusion.16), channel_id=1, replica_groups=mesh['prow'=8,'pcol'=32] {'prow'}, use_global_device_ids=true, to_apply=%region_3.0 | all-reduce | flops 8192 | bytes 65536 | tf_op jit(solution)/shard_map/psum | solution.py:25
  499.4 0.2 fusion
  499.7 10.1 %convolution_subtract_fusion = f32[64,12288]{1,0:T(8,128)} fusion(f32[64,12288]{1,0:T(8,128)S(1)} %convolution_subtract_fusion.1, f32[64,128]{1,0:T(8,128)S(1)} %fusion, f32[12288,128]{1,0:T(8,128)} %bitcast.6), kind=kOutput, calls=%fused_computation | convolution fusion | flops 1208745984 | bytes 12615680 | tf_op jit(solution)/shard_map/dot_general | solution.py:8
  (1 shorter events, 0.0 us)
Async XLA Ops:
  241.1 9.6 %copy-start.2 = (f32[64,12288]{1,0:T(8,128)S(1)}, f32[64,12288]{1,0:T(8,128)}, u32[]{:S(2)}) copy-start(f32[64,12288]{1,0:T(8,128)} %param.3) | copy-start | bytes 9437188
  241.1 225.0 %all-to-all-start.3 = ((f32[32,384,128]{2,1,0:T(8,128)}), f32[32,384,128]{2,1,0:T(8,128)}, u32[]{:S(2)}, u32[]{:S(2)}) async-start(f32[32,384,128]{2,1,0:T(8,128)} %stack.11), calls=%async_computation.3 | async-start | bytes 12582912 | tf_op jit(solution)/shard_map/all_to_all | solution.py:17
  250.7 118.4 %copy-start.3 = (f32[4,128,128]{2,1,0:T(8,128)S(1)}, f32[4,128,128]{2,1,0:T(8,128)}, u32[]{:S(2)}) copy-start(f32[4,128,128]{2,1,0:T(8,128)} %param.5) | copy-start | bytes 786436
  378.3 1.7 copy-start.1
  379.9 45.0 %slice-start = ((s8[6291456]{0:T(1024)(128)(4,1)}), s8[2097152]{0:T(1024)(128)(4,1)S(1)}, s32[]{:S(2)}) async-start(s8[6291456]{0:T(1024)(128)(4,1)} %bitcast.37), calls=%async_computation.4 | async-start | bytes 4194304
  413.7 11.3 %slice-start.1 = ((s8[6291456]{0:T(1024)(128)(4,1)}), s8[4194304]{0:T(1024)(128)(4,1)S(1)}, s32[]{:S(2)}) async-start(s8[6291456]{0:T(1024)(128)(4,1)} %bitcast.37), calls=%async_computation.5 | async-start | bytes 8388608
  423.3 1.7 copy-start
